TPU v7x, 32 devices: a whole 2x2x4 slice. The times are simulated.
32 devices in a mesh: gx: 16 (over z, y, x), gy: 2 (over core).
Axes of the slice: x: 2, y: 2, z: 4, core: 2. Of those that a mesh axis runs over, the one named last changes fastest.
Arguments:
- load_parts: bfloat16 [16, 2, 4, 192, 384], P('gx', 'gy'), may hold values from -6 to 6
- schur: bfloat16 [16, 2, 4, 384, 384], P('gx', 'gy'), may hold values from -4 to 4
- deluxe: bfloat16 [16, 2, 4, 384, 384], P('gx', 'gy'), may hold values from -4 to 4
- panels: bfloat16 [16, 2, 4, 384, 384], P('gx', 'gy'), may hold values from -4 to 4
- coarse_inverse: float32 [128, 128], P(('gx', 'gy')), may hold values from -1 to 1
- primal_dofs: int32 [16, 2, 4], P('gx', 'gy'), may hold values from 0 to 1535
- damage_flags: int32 [16, 2, 4], P('gx', 'gy'), may hold values 0 or 1
Outputs:
- increment: bfloat16 [16, 2, 4, 192, 384], P('gx', 'gy')
Inputs may be any that keep to these rules, and one draw needn't show every extreme that they name: `primal_dofs`: each entry names a face times 384 plus a position on that face.
All inputs are finite; a program needn't handle non-finite values. No bound on the sum of `damage_flags` on one device may be relied on, other than what follows from the above.
Results may differ from a plain program's by a relative error of at most 0.003.
The roundings to bfloat16 on the way count: a program that leaves them out, or rounds other values in their place, can miss the bound.
Values may be sent and summed in bfloat16 or wider, within the bound.
No kernel may reach another device: no remote copies, remote signals or barrier semaphores. Data moves between devices by JAX's collectives and lax.ppermute only.
A program may use at most 64 MiB of HBM per device.

v0:
```python
import jax
import jax.numpy as jnp
from jax import lax
from jax.sharding import PartitionSpec as P


def with_halo(block, sides, width):
    for axis, dim in sides:
        count = lax.axis_size(axis)
        forward = [(i, i + 1) for i in range(count - 1)]
        backward = [(target, source) for source, target in forward]
        low = lax.ppermute(
            lax.slice_in_dim(block, block.shape[dim] - width, None, axis=dim), axis, forward
        )
        high = lax.ppermute(lax.slice_in_dim(block, 0, width, axis=dim), axis, backward)
        block = jnp.concatenate([low, block, high], axis=dim)
    return block


def face_mul(vectors, matrices):
    return jnp.einsum("fry,fyx->frx", vectors, matrices, preferred_element_type=jnp.float32)


def face_mul_turned(vectors, matrices):
    return jnp.einsum("fry,fxy->frx", vectors, matrices, preferred_element_type=jnp.float32)


def face_pairs(values):
    along_first = with_halo(values[0:2], (("gx", 0),), 1)
    along_second = with_halo(values[2:4], (("gy", 0),), 1)
    return jnp.stack([along_first[0], along_first[3], along_second[0], along_second[3]], axis=0)


def image_pairs(values):
    along_first = with_halo(values[0:2], (("gx", 0),), 1)
    along_second = with_halo(values[2:4], (("gy", 0),), 1)
    return jnp.stack([along_first[0], along_first[3], along_second[0], along_second[3]], axis=0)


def per_device(load_parts, schur, deluxe, panels, coarse_inverse, primal_dofs, damage_flags):
    loads_here = load_parts[0, 0]
    schur_panel = schur[0, 0]
    deluxe_panel = deluxe[0, 0]
    inverse_panel = panels[0, 0]
    primal_slots = primal_dofs[0, 0]
    flag_values = damage_flags[0, 0]
    width = loads_here.shape[2]
    primal_count = primal_slots.shape[0]
    positions = jnp.arange(4 * width, dtype=jnp.int32)
    picks = (primal_slots[:, None] == positions[None, :]).reshape(primal_count, 4, width)
    picks_half = picks.astype(jnp.bfloat16)
    picks_full = picks.astype(jnp.float32)
    flags_full = flag_values.astype(jnp.float32)

    def add_coarse(piece):
        return jnp.dot(coarse_inverse, piece.astype(jnp.float32), precision=lax.Precision.HIGHEST)

    def precondition(resid):
        scaled = face_mul_turned(resid.astype(jnp.bfloat16), deluxe_panel).astype(jnp.bfloat16)
        local_part = face_mul(scaled, inverse_panel)
        extra = face_mul(local_part.astype(jnp.bfloat16), inverse_panel)
        softened = local_part + 0.5 * flags_full[:, None, None] * extra
        primal = jnp.einsum(
            "kfx,frx->kr", picks_half, scaled, preferred_element_type=jnp.float32
        ).astype(jnp.bfloat16)
        coarse = add_coarse(lax.all_gather(primal, ("gx", "gy"), axis=0, tiled=True))
        placed = jnp.einsum("kfx,kr->frx", picks_full, coarse, precision=lax.Precision.HIGHEST)
        weighted = (softened + placed).astype(jnp.bfloat16)
        spread = face_mul(weighted, deluxe_panel).astype(jnp.bfloat16)
        return spread.astype(jnp.float32) + face_pairs(spread).astype(jnp.float32)

    def apply_operator(field):
        bent = face_mul(field.astype(jnp.bfloat16), schur_panel).astype(jnp.bfloat16)
        return bent.astype(jnp.float32) + image_pairs(bent).astype(jnp.float32)

    resid0 = loads_here.astype(jnp.float32) + face_pairs(loads_here).astype(jnp.float32)
    first = precondition(resid0)
    resid1 = resid0 - apply_operator(first)
    second = precondition(resid1)
    top = lax.psum(jnp.sum(resid1 * second, axis=(0, 2)), ("gx", "gy"))
    curved = apply_operator(second)
    bottom = lax.psum(jnp.sum(second * curved, axis=(0, 2)), ("gx", "gy"))
    step_len = top / bottom
    result = (first + step_len[:, None] * second).astype(jnp.bfloat16)
    return result[None, None]


def solution(mesh):
    return jax.shard_map(
        per_device,
        mesh=mesh,
        in_specs=(
            P("gx", "gy", None, None, None),
            P("gx", "gy", None, None, None),
            P("gx", "gy", None, None, None),
            P("gx", "gy", None, None, None),
            P(("gx", "gy"), None),
            P("gx", "gy", None),
            P("gx", "gy", None),
        ),
        out_specs=P("gx", "gy", None, None, None),
        check_vma=False,
    )
```

profile of v0, /device:TPU:10, one launch (start us, length us, event | category | flops | bytes accessed | tf_op | source)
XLA Modules:
  0.0 210.2 jit_solution(9755467577524988544)
XLA Ops:
  0.0 1.3 slice_bitcast_fusion.3
  1.3 3.4 %collective-permute-start = (bf16[1,192,384]{2,1,0:T(8,128)(2,1)S(1)}, bf16[1,192,384]{2,1,0:T(8,128)(2,1)S(1)}, u32[]{:S(2)}, u32[]{:S(2)}) collective-permute-start(bf16[1,192,384]{2,1,0:T(8,128)(2,1)S(1)} %get-tuple-element.23), channel_id=1, source_target_pairs={{0,2},{2,4},{4,6},{6,8},{8,10},{10,12},{12,14},{14,16},{16,18},{18... | collective-permute-start | bytes 442376 | tf_op jit(solution)/shard_map/ppermute | solution.py:12
  4.7 2.4 %collective-permute-start.1 = (bf16[1,192,384]{2,1,0:T(8,128)(2,1)S(1)}, bf16[1,192,384]{2,1,0:T(8,128)(2,1)S(1)}, u32[]{:S(2)}, u32[]{:S(2)}) collective-permute-start(bf16[1,192,384]{2,1,0:T(8,128)(2,1)S(1)} %get-tuple-element.24), channel_id=1, source_target_pairs={{2,0},{4,2},{6,4},{8,6},{10,8},{12,10},{14,12},{16,14},{18,16},{20... | collective-permute-start | bytes 442376 | tf_op jit(solution)/shard_map/ppermute | solution.py:15
  8.5 3.0 %collective-permute-start.2 = (bf16[1,192,384]{2,1,0:T(8,128)(2,1)S(1)}, bf16[1,192,384]{2,1,0:T(8,128)(2,1)S(1)}, u32[]{:S(2)}, u32[]{:S(2)}) collective-permute-start(bf16[1,192,384]{2,1,0:T(8,128)(2,1)S(1)} %get-tuple-element.26), channel_id=1, source_target_pairs={{0,1},{2,3},{4,5},{6,7},{8,9},{10,11},{12,13},{14,15},{16,17},{18,... | collective-permute-start | bytes 442376 | tf_op jit(solution)/shard_map/ppermute | solution.py:12
  14.0 34.1 %all-gather = bf16[32,4,192]{2,1,0:T(4,128)(2,1)} all-gather(bf16[1,4,192]{2,1,0:T(4,128)(2,1)S(1)} %fusion.25), channel_id=1, replica_groups=mesh['gx'=16,'gy'=2] {'gx','gy'}, dimensions={0}, use_global_device_ids=true | all-gather | bytes 50688 | tf_op jit(solution)/shard_map/all_gather | solution.py:66
  48.0 1.5 reshape.37
  49.6 1.5 fusion.14
  51.2 1.8 convolution_bitcast_fusion.1
  53.0 2.9 %convolution_convert_fusion.4 = bf16[4,192,384]{2,1,0:T(8,128)(2,1)S(1)} fusion(f32[4,192,384]{2,1,0:T(8,128)} %convolution_bitcast_fusion.1, f32[4,192,384]{2,1,0:T(8,128)} %fusion.14, bf16[1,1,4,384,384]{4,3,2,1,0:T(8,128)(2,1)S(1)} %copy-done.1, bf16[1,1,4,384,384]{4,3,2,1,0:T(8,128)(2,1)S(1)} %copy-done, f32[4]{0:T(128)} %multiply_bitcast_fusion), kind=kOutput, calls=%fused_computation.14 | convolution fusion | flops 454754304 | bytes 5308432 | tf_op jit(solution)/shard_map/fry,fyx->frx/dot_general | solution.py:21
  56.0 3.5 %collective-permute-start.4 = (bf16[1,192,384]{2,1,0:T(8,128)(2,1)S(1)}, bf16[1,192,384]{2,1,0:T(8,128)(2,1)S(1)}, u32[]{:S(2)}, u32[]{:S(2)}) collective-permute-start(bf16[1,192,384]{2,1,0:T(8,128)(2,1)S(1)} %get-tuple-element.19), channel_id=1, source_target_pairs={{0,2},{2,4},{4,6},{6,8},{8,10},{10,12},{12,14},{14,16},{16,18},{18... | collective-permute-start | bytes 442376 | tf_op jit(solution)/shard_map/ppermute | solution.py:12
  59.5 1.3 collective-permute-start.7
  60.8 3.0 %collective-permute-start.6 = (bf16[1,192,384]{2,1,0:T(8,128)(2,1)S(1)}, bf16[1,192,384]{2,1,0:T(8,128)(2,1)S(1)}, u32[]{:S(2)}, u32[]{:S(2)}) collective-permute-start(bf16[1,192,384]{2,1,0:T(8,128)(2,1)S(1)} %get-tuple-element.21), channel_id=1, source_target_pairs={{0,1},{2,3},{4,5},{6,7},{8,9},{10,11},{12,13},{14,15},{16,17},{18,... | collective-permute-start | bytes 442376 | tf_op jit(solution)/shard_map/ppermute | solution.py:12
  63.9 4.6 %collective-permute-start.5 = (bf16[1,192,384]{2,1,0:T(8,128)(2,1)S(1)}, bf16[1,192,384]{2,1,0:T(8,128)(2,1)S(1)}, u32[]{:S(2)}, u32[]{:S(2)}) collective-permute-start(bf16[1,192,384]{2,1,0:T(8,128)(2,1)S(1)} %get-tuple-element.22), channel_id=1, source_target_pairs={{2,0},{4,2},{6,4},{8,6},{10,8},{12,10},{14,12},{16,14},{18,16},{20... | collective-permute-start | bytes 442376 | tf_op jit(solution)/shard_map/ppermute | solution.py:15
  68.6 3.3 %collective-permute-done.5 = bf16[1,192,384]{2,1,0:T(8,128)(2,1)S(1)} collective-permute-done((bf16[1,192,384]{2,1,0:T(8,128)(2,1)S(1)}, bf16[1,192,384]{2,1,0:T(8,128)(2,1)S(1)}, u32[]{:S(2)}, u32[]{:S(2)}) %collective-permute-start.5) | collective-permute-done | bytes 147488 | tf_op jit(solution)/shard_map/ppermute | solution.py:15
  72.6 3.5 %collective-permute-start.8 = (bf16[1,192,384]{2,1,0:T(8,128)(2,1)S(1)}, bf16[1,192,384]{2,1,0:T(8,128)(2,1)S(1)}, u32[]{:S(2)}, u32[]{:S(2)}) collective-permute-start(bf16[1,192,384]{2,1,0:T(8,128)(2,1)S(1)} %get-tuple-element.15), channel_id=1, source_target_pairs={{0,2},{2,4},{4,6},{6,8},{8,10},{10,12},{12,14},{14,16},{16,18},{18... | collective-permute-start | bytes 442376 | tf_op jit(solution)/shard_map/ppermute | solution.py:12
  77.4 3.0 %collective-permute-start.10 = (bf16[1,192,384]{2,1,0:T(8,128)(2,1)S(1)}, bf16[1,192,384]{2,1,0:T(8,128)(2,1)S(1)}, u32[]{:S(2)}, u32[]{:S(2)}) collective-permute-start(bf16[1,192,384]{2,1,0:T(8,128)(2,1)S(1)} %get-tuple-element.17), channel_id=1, source_target_pairs={{0,1},{2,3},{4,5},{6,7},{8,9},{10,11},{12,13},{14,15},{16,17},{18,... | collective-permute-start | bytes 442376 | tf_op jit(solution)/shard_map/ppermute | solution.py:12
  80.4 3.6 %collective-permute-start.9 = (bf16[1,192,384]{2,1,0:T(8,128)(2,1)S(1)}, bf16[1,192,384]{2,1,0:T(8,128)(2,1)S(1)}, u32[]{:S(2)}, u32[]{:S(2)}) collective-permute-start(bf16[1,192,384]{2,1,0:T(8,128)(2,1)S(1)} %get-tuple-element.18), channel_id=1, source_target_pairs={{2,0},{4,2},{6,4},{8,6},{10,8},{12,10},{14,12},{16,14},{18,16},{20... | collective-permute-start | bytes 442376 | tf_op jit(solution)/shard_map/ppermute | solution.py:15
  84.1 5.0 %collective-permute-done.9 = bf16[1,192,384]{2,1,0:T(8,128)(2,1)S(1)} collective-permute-done((bf16[1,192,384]{2,1,0:T(8,128)(2,1)S(1)}, bf16[1,192,384]{2,1,0:T(8,128)(2,1)S(1)}, u32[]{:S(2)}, u32[]{:S(2)}) %collective-permute-start.9) | collective-permute-done | bytes 147488 | tf_op jit(solution)/shard_map/ppermute | solution.py:15
  90.2 1.6 fusion.10
  91.7 35.3 %all-gather.1 = bf16[32,4,192]{2,1,0:T(4,128)(2,1)S(1)} all-gather(bf16[1,4,192]{2,1,0:T(4,128)(2,1)S(1)} %fusion.24), channel_id=1, replica_groups=mesh['gx'=16,'gy'=2] {'gx','gy'}, dimensions={0}, use_global_device_ids=true | all-gather | bytes 50688 | tf_op jit(solution)/shard_map/all_gather | solution.py:66
  127.2 1.8 convolution_bitcast_fusion
  129.0 2.9 %convolution_convert_fusion.1 = bf16[4,192,384]{2,1,0:T(8,128)(2,1)S(1)} fusion(f32[4,192,384]{2,1,0:T(8,128)} %convolution_bitcast_fusion, f32[4,192,384]{2,1,0:T(8,128)} %fusion.10, bf16[1,1,4,384,384]{4,3,2,1,0:T(8,128)(2,1)S(1)} %copy-done.1, bf16[1,1,4,384,384]{4,3,2,1,0:T(8,128)(2,1)S(1)} %copy-done, f32[4]{0:T(128)} %multiply_bitcast_fusion), kind=kOutput, calls=%fused_computation.11 | convolution fusion | flops 454754304 | bytes 5308432 | tf_op jit(solution)/shard_map/fry,fyx->frx/dot_general | solution.py:21
  132.0 2.1 collective-permute-start.12
  135.4 3.0 %collective-permute-start.14 = (bf16[1,192,384]{2,1,0:T(8,128)(2,1)S(1)}, bf16[1,192,384]{2,1,0:T(8,128)(2,1)S(1)}, u32[]{:S(2)}, u32[]{:S(2)}) collective-permute-start(bf16[1,192,384]{2,1,0:T(8,128)(2,1)S(1)} %get-tuple-element.13), channel_id=1, source_target_pairs={{0,1},{2,3},{4,5},{6,7},{8,9},{10,11},{12,13},{14,15},{16,17},{18,... | collective-permute-start | bytes 442376 | tf_op jit(solution)/shard_map/ppermute | solution.py:12
  138.4 3.9 %collective-permute-start.13 = (bf16[1,192,384]{2,1,0:T(8,128)(2,1)S(1)}, bf16[1,192,384]{2,1,0:T(8,128)(2,1)S(1)}, u32[]{:S(2)}, u32[]{:S(2)}) collective-permute-start(bf16[1,192,384]{2,1,0:T(8,128)(2,1)S(1)} %get-tuple-element.14), channel_id=1, source_target_pairs={{2,0},{4,2},{6,4},{8,6},{10,8},{12,10},{14,12},{16,14},{18,16},{20... | collective-permute-start | bytes 442376 | tf_op jit(solution)/shard_map/ppermute | solution.py:15
  142.4 3.9 %collective-permute-done.13 = bf16[1,192,384]{2,1,0:T(8,128)(2,1)S(1)} collective-permute-done((bf16[1,192,384]{2,1,0:T(8,128)(2,1)S(1)}, bf16[1,192,384]{2,1,0:T(8,128)(2,1)S(1)}, u32[]{:S(2)}, u32[]{:S(2)}) %collective-permute-start.13) | collective-permute-done | bytes 147488 | tf_op jit(solution)/shard_map/ppermute | solution.py:15
  147.1 2.9 %collective-permute-start.16 = (bf16[1,192,384]{2,1,0:T(8,128)(2,1)S(1)}, bf16[1,192,384]{2,1,0:T(8,128)(2,1)S(1)}, u32[]{:S(2)}, u32[]{:S(2)}) collective-permute-start(bf16[1,192,384]{2,1,0:T(8,128)(2,1)S(1)} %get-tuple-element.7), channel_id=1, source_target_pairs={{0,2},{2,4},{4,6},{6,8},{8,10},{10,12},{12,14},{14,16},{16,18},{18... | collective-permute-start | bytes 442376 | tf_op jit(solution)/shard_map/ppermute | solution.py:12
  151.2 3.0 %collective-permute-start.18 = (bf16[1,192,384]{2,1,0:T(8,128)(2,1)S(1)}, bf16[1,192,384]{2,1,0:T(8,128)(2,1)S(1)}, u32[]{:S(2)}, u32[]{:S(2)}) collective-permute-start(bf16[1,192,384]{2,1,0:T(8,128)(2,1)S(1)} %get-tuple-element.9), channel_id=1, source_target_pairs={{0,1},{2,3},{4,5},{6,7},{8,9},{10,11},{12,13},{14,15},{16,17},{18,... | collective-permute-start | bytes 442376 | tf_op jit(solution)/shard_map/ppermute | solution.py:12
  154.3 3.4 %collective-permute-start.17 = (bf16[1,192,384]{2,1,0:T(8,128)(2,1)S(1)}, bf16[1,192,384]{2,1,0:T(8,128)(2,1)S(1)}, u32[]{:S(2)}, u32[]{:S(2)}) collective-permute-start(bf16[1,192,384]{2,1,0:T(8,128)(2,1)S(1)} %get-tuple-element.10), channel_id=1, source_target_pairs={{2,0},{4,2},{6,4},{8,6},{10,8},{12,10},{14,12},{16,14},{18,16},{20... | collective-permute-start | bytes 442376 | tf_op jit(solution)/shard_map/ppermute | solution.py:15
  158.4 3.8 %collective-permute-done.17 = bf16[1,192,384]{2,1,0:T(8,128)(2,1)S(1)} collective-permute-done((bf16[1,192,384]{2,1,0:T(8,128)(2,1)S(1)}, bf16[1,192,384]{2,1,0:T(8,128)(2,1)S(1)}, u32[]{:S(2)}, u32[]{:S(2)}) %collective-permute-start.17) | collective-permute-done | bytes 147488 | tf_op jit(solution)/shard_map/ppermute | solution.py:15
  162.6 45.2 %all-reduce = (f32[192]{0:T(256)S(1)}, f32[192]{0:T(256)S(1)}) all-reduce(f32[192]{0:T(256)S(1)} %multiply_reduce_fusion.1, f32[192]{0:T(256)S(1)} %multiply_reduce_fusion), channel_id=1, replica_groups=mesh['gx'=16,'gy'=2] {'gx','gy'}, use_global_device_ids=true, to_apply=%region_1.0 | all-reduce | flops 384 | bytes 3072 | tf_op jit(solution)/shard_map/psum | solution.py:80
  207.9 2.3 %fusion.30 = bf16[1,1,4,192,384]{4,3,2,1,0:T(8,128)(2,1)} fusion(bf16[4,192,384]{2,1,0:T(8,128)(2,1)S(1)} %convolution_convert_fusion.1, bf16[4,192,384]{2,1,0:T(8,128)(2,1)S(1)} %convolution_convert_fusion.4, f32[192]{0:T(256)S(1)} %div.3, bf16[1,192,384]{2,1,0:T(8,128)(2,1)S(1)} %copy-done.26, bf16[1,192,384]{2,1,0:T(8,128)(2,1)S(1)} %copy-done.28, ...), kind=kLoop, calls=%fused_computation.46 | loop fusion | flops 4423680 | bytes 2949888 | tf_op jit(solution)/shard_map/broadcast_in_dim | solution.py:85
  (126 shorter events, 11.3 us)
Async XLA Ops:
  1.3 10.8 %collective-permute-start = (bf16[1,192,384]{2,1,0:T(8,128)(2,1)S(1)}, bf16[1,192,384]{2,1,0:T(8,128)(2,1)S(1)}, u32[]{:S(2)}, u32[]{:S(2)}) collective-permute-start(bf16[1,192,384]{2,1,0:T(8,128)(2,1)S(1)} %get-tuple-element.23), channel_id=1, source_target_pairs={{0,2},{2,4},{4,6},{6,8},{8,10},{10,12},{12,14},{14,16},{16,18},{18... | collective-permute-start | bytes 442376 | tf_op jit(solution)/shard_map/ppermute | solution.py:12
  4.7 8.2 %collective-permute-start.1 = (bf16[1,192,384]{2,1,0:T(8,128)(2,1)S(1)}, bf16[1,192,384]{2,1,0:T(8,128)(2,1)S(1)}, u32[]{:S(2)}, u32[]{:S(2)}) collective-permute-start(bf16[1,192,384]{2,1,0:T(8,128)(2,1)S(1)} %get-tuple-element.24), channel_id=1, source_target_pairs={{2,0},{4,2},{6,4},{8,6},{10,8},{12,10},{14,12},{16,14},{18,16},{20... | collective-permute-start | bytes 442376 | tf_op jit(solution)/shard_map/ppermute | solution.py:15
  7.2 5.7 %collective-permute-start.3 = (bf16[1,192,384]{2,1,0:T(8,128)(2,1)S(1)}, bf16[1,192,384]{2,1,0:T(8,128)(2,1)S(1)}, u32[]{:S(2)}, u32[]{:S(2)}) collective-permute-start(bf16[1,192,384]{2,1,0:T(8,128)(2,1)S(1)} %get-tuple-element.25), channel_id=1, source_target_pairs={{1,0},{3,2},{5,4},{7,6},{9,8},{11,10},{13,12},{15,14},{17,16},{19,... | collective-permute-start | bytes 442376 | tf_op jit(solution)/shard_map/ppermute | solution.py:15
  8.5 4.5 %collective-permute-start.2 = (bf16[1,192,384]{2,1,0:T(8,128)(2,1)S(1)}, bf16[1,192,384]{2,1,0:T(8,128)(2,1)S(1)}, u32[]{:S(2)}, u32[]{:S(2)}) collective-permute-start(bf16[1,192,384]{2,1,0:T(8,128)(2,1)S(1)} %get-tuple-element.26), channel_id=1, source_target_pairs={{0,1},{2,3},{4,5},{6,7},{8,9},{10,11},{12,13},{14,15},{16,17},{18,... | collective-permute-start | bytes 442376 | tf_op jit(solution)/shard_map/ppermute | solution.py:12
  13.0 36.6 %copy-start.1 = (bf16[1,1,4,384,384]{4,3,2,1,0:T(8,128)(2,1)S(1)}, bf16[1,1,4,384,384]{4,3,2,1,0:T(8,128)(2,1)}, u32[]{:S(2)}) copy-start(bf16[1,1,4,384,384]{4,3,2,1,0:T(8,128)(2,1)} %param.10) | copy-start | bytes 3538948
  56.0 12.5 %collective-permute-start.4 = (bf16[1,192,384]{2,1,0:T(8,128)(2,1)S(1)}, bf16[1,192,384]{2,1,0:T(8,128)(2,1)S(1)}, u32[]{:S(2)}, u32[]{:S(2)}) collective-permute-start(bf16[1,192,384]{2,1,0:T(8,128)(2,1)S(1)} %get-tuple-element.19), channel_id=1, source_target_pairs={{0,2},{2,4},{4,6},{6,8},{8,10},{10,12},{12,14},{14,16},{16,18},{18... | collective-permute-start | bytes 442376 | tf_op jit(solution)/shard_map/ppermute | solution.py:12
  59.5 9.0 %collective-permute-start.7 = (bf16[1,192,384]{2,1,0:T(8,128)(2,1)S(1)}, bf16[1,192,384]{2,1,0:T(8,128)(2,1)S(1)}, u32[]{:S(2)}, u32[]{:S(2)}) collective-permute-start(bf16[1,192,384]{2,1,0:T(8,128)(2,1)S(1)} %get-tuple-element.20), channel_id=1, source_target_pairs={{1,0},{3,2},{5,4},{7,6},{9,8},{11,10},{13,12},{15,14},{17,16},{19,... | collective-permute-start | bytes 442376 | tf_op jit(solution)/shard_map/ppermute | solution.py:15
  60.8 7.7 %collective-permute-start.6 = (bf16[1,192,384]{2,1,0:T(8,128)(2,1)S(1)}, bf16[1,192,384]{2,1,0:T(8,128)(2,1)S(1)}, u32[]{:S(2)}, u32[]{:S(2)}) collective-permute-start(bf16[1,192,384]{2,1,0:T(8,128)(2,1)S(1)} %get-tuple-element.21), channel_id=1, source_target_pairs={{0,1},{2,3},{4,5},{6,7},{8,9},{10,11},{12,13},{14,15},{16,17},{18,... | collective-permute-start | bytes 442376 | tf_op jit(solution)/shard_map/ppermute | solution.py:12
  63.9 7.9 %collective-permute-start.5 = (bf16[1,192,384]{2,1,0:T(8,128)(2,1)S(1)}, bf16[1,192,384]{2,1,0:T(8,128)(2,1)S(1)}, u32[]{:S(2)}, u32[]{:S(2)}) collective-permute-start(bf16[1,192,384]{2,1,0:T(8,128)(2,1)S(1)} %get-tuple-element.22), channel_id=1, source_target_pairs={{2,0},{4,2},{6,4},{8,6},{10,8},{12,10},{14,12},{16,14},{18,16},{20... | collective-permute-start | bytes 442376 | tf_op jit(solution)/shard_map/ppermute | solution.py:15
  72.5 17.4 %copy-start.4 = (bf16[4,192,384]{2,1,0:T(8,128)(2,1)}, bf16[4,192,384]{2,1,0:T(8,128)(2,1)S(1)}, u32[]{:S(2)}) copy-start(bf16[4,192,384]{2,1,0:T(8,128)(2,1)S(1)} %convolution_convert_fusion.3) | copy-start | bytes 1769476
  72.5 16.7 %copy-start.15 = (bf16[1,192,384]{2,1,0:T(8,128)(2,1)S(1)}, bf16[1,192,384]{2,1,0:T(8,128)(2,1)}, u32[]{:S(2)}) copy-start(bf16[1,192,384]{2,1,0:T(8,128)(2,1)} %copy-done.14) | copy-start | bytes 442372
  72.5 16.7 %copy-start.18 = (bf16[1,192,384]{2,1,0:T(8,128)(2,1)S(1)}, bf16[1,192,384]{2,1,0:T(8,128)(2,1)}, u32[]{:S(2)}) copy-start(bf16[1,192,384]{2,1,0:T(8,128)(2,1)} %copy-done.17) | copy-start | bytes 442372
  72.5 16.7 %copy-start.21 = (bf16[1,192,384]{2,1,0:T(8,128)(2,1)S(1)}, bf16[1,192,384]{2,1,0:T(8,128)(2,1)}, u32[]{:S(2)}) copy-start(bf16[1,192,384]{2,1,0:T(8,128)(2,1)} %copy-done.20) | copy-start | bytes 442372
  72.6 11.5 %collective-permute-start.8 = (bf16[1,192,384]{2,1,0:T(8,128)(2,1)S(1)}, bf16[1,192,384]{2,1,0:T(8,128)(2,1)S(1)}, u32[]{:S(2)}, u32[]{:S(2)}) collective-permute-start(bf16[1,192,384]{2,1,0:T(8,128)(2,1)S(1)} %get-tuple-element.15), channel_id=1, source_target_pairs={{0,2},{2,4},{4,6},{6,8},{8,10},{10,12},{12,14},{14,16},{16,18},{18... | collective-permute-start | bytes 442376 | tf_op jit(solution)/shard_map/ppermute | solution.py:12
  76.1 8.0 %collective-permute-start.11 = (bf16[1,192,384]{2,1,0:T(8,128)(2,1)S(1)}, bf16[1,192,384]{2,1,0:T(8,128)(2,1)S(1)}, u32[]{:S(2)}, u32[]{:S(2)}) collective-permute-start(bf16[1,192,384]{2,1,0:T(8,128)(2,1)S(1)} %get-tuple-element.16), channel_id=1, source_target_pairs={{1,0},{3,2},{5,4},{7,6},{9,8},{11,10},{13,12},{15,14},{17,16},{19,... | collective-permute-start | bytes 442376 | tf_op jit(solution)/shard_map/ppermute | solution.py:15
  77.4 6.7 %collective-permute-start.10 = (bf16[1,192,384]{2,1,0:T(8,128)(2,1)S(1)}, bf16[1,192,384]{2,1,0:T(8,128)(2,1)S(1)}, u32[]{:S(2)}, u32[]{:S(2)}) collective-permute-start(bf16[1,192,384]{2,1,0:T(8,128)(2,1)S(1)} %get-tuple-element.17), channel_id=1, source_target_pairs={{0,1},{2,3},{4,5},{6,7},{8,9},{10,11},{12,13},{14,15},{16,17},{18,... | collective-permute-start | bytes 442376 | tf_op jit(solution)/shard_map/ppermute | solution.py:12
  80.4 8.7 %collective-permute-start.9 = (bf16[1,192,384]{2,1,0:T(8,128)(2,1)S(1)}, bf16[1,192,384]{2,1,0:T(8,128)(2,1)S(1)}, u32[]{:S(2)}, u32[]{:S(2)}) collective-permute-start(bf16[1,192,384]{2,1,0:T(8,128)(2,1)S(1)} %get-tuple-element.18), channel_id=1, source_target_pairs={{2,0},{4,2},{6,4},{8,6},{10,8},{12,10},{14,12},{16,14},{18,16},{20... | collective-permute-start | bytes 442376 | tf_op jit(solution)/shard_map/ppermute | solution.py:15
  132.0 10.3 %collective-permute-start.12 = (bf16[1,192,384]{2,1,0:T(8,128)(2,1)S(1)}, bf16[1,192,384]{2,1,0:T(8,128)(2,1)S(1)}, u32[]{:S(2)}, u32[]{:S(2)}) collective-permute-start(bf16[1,192,384]{2,1,0:T(8,128)(2,1)S(1)} %get-tuple-element.11), channel_id=1, source_target_pairs={{0,2},{2,4},{4,6},{6,8},{8,10},{10,12},{12,14},{14,16},{16,18},{18... | collective-permute-start | bytes 442376 | tf_op jit(solution)/shard_map/ppermute | solution.py:12
  134.1 8.3 %collective-permute-start.15 = (bf16[1,192,384]{2,1,0:T(8,128)(2,1)S(1)}, bf16[1,192,384]{2,1,0:T(8,128)(2,1)S(1)}, u32[]{:S(2)}, u32[]{:S(2)}) collective-permute-start(bf16[1,192,384]{2,1,0:T(8,128)(2,1)S(1)} %get-tuple-element.12), channel_id=1, source_target_pairs={{1,0},{3,2},{5,4},{7,6},{9,8},{11,10},{13,12},{15,14},{17,16},{19,... | collective-permute-start | bytes 442376 | tf_op jit(solution)/shard_map/ppermute | solution.py:15
  135.4 7.0 %collective-permute-start.14 = (bf16[1,192,384]{2,1,0:T(8,128)(2,1)S(1)}, bf16[1,192,384]{2,1,0:T(8,128)(2,1)S(1)}, u32[]{:S(2)}, u32[]{:S(2)}) collective-permute-start(bf16[1,192,384]{2,1,0:T(8,128)(2,1)S(1)} %get-tuple-element.13), channel_id=1, source_target_pairs={{0,1},{2,3},{4,5},{6,7},{8,9},{10,11},{12,13},{14,15},{16,17},{18,... | collective-permute-start | bytes 442376 | tf_op jit(solution)/shard_map/ppermute | solution.py:12
  138.4 7.9 %collective-permute-start.13 = (bf16[1,192,384]{2,1,0:T(8,128)(2,1)S(1)}, bf16[1,192,384]{2,1,0:T(8,128)(2,1)S(1)}, u32[]{:S(2)}, u32[]{:S(2)}) collective-permute-start(bf16[1,192,384]{2,1,0:T(8,128)(2,1)S(1)} %get-tuple-element.14), channel_id=1, source_target_pairs={{2,0},{4,2},{6,4},{8,6},{10,8},{12,10},{14,12},{16,14},{18,16},{20... | collective-permute-start | bytes 442376 | tf_op jit(solution)/shard_map/ppermute | solution.py:15
  142.4 19.9 %copy-start.6 = (bf16[1,192,384]{2,1,0:T(8,128)(2,1)}, bf16[1,192,384]{2,1,0:T(8,128)(2,1)S(1)}, u32[]{:S(2)}) copy-start(bf16[1,192,384]{2,1,0:T(8,128)(2,1)S(1)} %collective-permute-done.12) | copy-start | bytes 442372
  142.4 19.8 %copy-start.7 = (bf16[1,192,384]{2,1,0:T(8,128)(2,1)}, bf16[1,192,384]{2,1,0:T(8,128)(2,1)S(1)}, u32[]{:S(2)}) copy-start(bf16[1,192,384]{2,1,0:T(8,128)(2,1)S(1)} %collective-permute-done.15) | copy-start | bytes 442372
  142.4 19.8 %copy-start.8 = (bf16[1,192,384]{2,1,0:T(8,128)(2,1)}, bf16[1,192,384]{2,1,0:T(8,128)(2,1)S(1)}, u32[]{:S(2)}) copy-start(bf16[1,192,384]{2,1,0:T(8,128)(2,1)S(1)} %collective-permute-done.14) | copy-start | bytes 442372
  147.1 11.3 %collective-permute-start.16 = (bf16[1,192,384]{2,1,0:T(8,128)(2,1)S(1)}, bf16[1,192,384]{2,1,0:T(8,128)(2,1)S(1)}, u32[]{:S(2)}, u32[]{:S(2)}) collective-permute-start(bf16[1,192,384]{2,1,0:T(8,128)(2,1)S(1)} %get-tuple-element.7), channel_id=1, source_target_pairs={{0,2},{2,4},{4,6},{6,8},{8,10},{10,12},{12,14},{14,16},{16,18},{18... | collective-permute-start | bytes 442376 | tf_op jit(solution)/shard_map/ppermute | solution.py:12
  149.9 8.4 %collective-permute-start.19 = (bf16[1,192,384]{2,1,0:T(8,128)(2,1)S(1)}, bf16[1,192,384]{2,1,0:T(8,128)(2,1)S(1)}, u32[]{:S(2)}, u32[]{:S(2)}) collective-permute-start(bf16[1,192,384]{2,1,0:T(8,128)(2,1)S(1)} %get-tuple-element.8), channel_id=1, source_target_pairs={{1,0},{3,2},{5,4},{7,6},{9,8},{11,10},{13,12},{15,14},{17,16},{19,... | collective-permute-start | bytes 442376 | tf_op jit(solution)/shard_map/ppermute | solution.py:15
  151.2 7.1 %collective-permute-start.18 = (bf16[1,192,384]{2,1,0:T(8,128)(2,1)S(1)}, bf16[1,192,384]{2,1,0:T(8,128)(2,1)S(1)}, u32[]{:S(2)}, u32[]{:S(2)}) collective-permute-start(bf16[1,192,384]{2,1,0:T(8,128)(2,1)S(1)} %get-tuple-element.9), channel_id=1, source_target_pairs={{0,1},{2,3},{4,5},{6,7},{8,9},{10,11},{12,13},{14,15},{16,17},{18,... | collective-permute-start | bytes 442376 | tf_op jit(solution)/shard_map/ppermute | solution.py:12
  154.3 7.9 %collective-permute-start.17 = (bf16[1,192,384]{2,1,0:T(8,128)(2,1)S(1)}, bf16[1,192,384]{2,1,0:T(8,128)(2,1)S(1)}, u32[]{:S(2)}, u32[]{:S(2)}) collective-permute-start(bf16[1,192,384]{2,1,0:T(8,128)(2,1)S(1)} %get-tuple-element.10), channel_id=1, source_target_pairs={{2,0},{4,2},{6,4},{8,6},{10,8},{12,10},{14,12},{16,14},{18,16},{20... | collective-permute-start | bytes 442376 | tf_op jit(solution)/shard_map/ppermute | solution.py:15
  158.3 49.5 %copy-start.24 = (bf16[1,192,384]{2,1,0:T(8,128)(2,1)S(1)}, bf16[1,192,384]{2,1,0:T(8,128)(2,1)}, u32[]{:S(2)}) copy-start(bf16[1,192,384]{2,1,0:T(8,128)(2,1)} %copy-done.23) | copy-start | bytes 442372
  158.3 49.5 %copy-start.26 = (bf16[1,192,384]{2,1,0:T(8,128)(2,1)S(1)}, bf16[1,192,384]{2,1,0:T(8,128)(2,1)}, u32[]{:S(2)}) copy-start(bf16[1,192,384]{2,1,0:T(8,128)(2,1)} %copy-done.25) | copy-start | bytes 442372
  158.3 49.5 %copy-start.28 = (bf16[1,192,384]{2,1,0:T(8,128)(2,1)S(1)}, bf16[1,192,384]{2,1,0:T(8,128)(2,1)}, u32[]{:S(2)}) copy-start(bf16[1,192,384]{2,1,0:T(8,128)(2,1)} %copy-done.27) | copy-start | bytes 442372
  158.4 49.5 %copy-start.30 = (bf16[1,192,384]{2,1,0:T(8,128)(2,1)S(1)}, bf16[1,192,384]{2,1,0:T(8,128)(2,1)}, u32[]{:S(2)}) copy-start(bf16[1,192,384]{2,1,0:T(8,128)(2,1)} %copy-done.29) | copy-start | bytes 442372
  (32 other events, 250.7 us)
where the time goes:
time: 211 us; the launch traced here: 210 us
  blocking collectives  115 us (55%)
  starting transfers between devices  55 us (26%)
  waiting for transfers between devices  16.9 us (8%)
  matrix products  15.6 us (7%)
  other arithmetic  3.87 us (2%)
  local copies, waits for them, and re-layouts  3.46 us (2%)
    all_gather x2, blocking collectives, precondition(): lax.all_gather(primal, ('gx', 'gy'), axis=0, tiled=True)  69.4 us
    psum x1, blocking collectives, per_device(): top = lax.psum(jnp.sum(resid1 * second, axis=(0, 2)), ('gx', 'gy'))  45.2 us
    ppermute x10, starting transfers between devices, with_halo(): lax.ppermute(lax.slice_in_dim(block, block.shape[dim] - width, None, axis...  30.5 us
    ppermute x10, starting transfers between devices, with_halo(): lax.ppermute(lax.slice_in_dim(block, 0, width, axis=dim), axis, backward)  24.4 us
    ppermute x10, waiting for transfers between devices, with_halo(): lax.ppermute(lax.slice_in_dim(block, 0, width, axis=dim), axis, backward)  16.8 us
    dot_general x6, matrix products, face_mul(): jnp.einsum('fry,fyx->frx', vectors, matrices, preferred_element_type=jnp....  9.97 us
  transfers between devices with their start and end apart: 20, of which 5 were waited for; matrix products, arithmetic and copies ran while one was open for 1% of the time, Pallas kernels for 0%

commit v1 on v0

--- a/solution.py
+++ b/solution.py
@@ -1,7 +1,17 @@
+import functools
 import jax
 import jax.numpy as jnp
 from jax import lax
 from jax.sharding import PartitionSpec as P
+
+
+def switch_face_over_axis(point, bus_axis, peer_axis):
+    for idx in (bus_axis, peer_axis):
+        point = jax.lax.psum(point, idx)
+    return point
+
+
+block_cut = functools.partial(switch_face_over_axis, bus_axis="gy", peer_axis="gx")
 
 
 def with_halo(block, sides, width):
@@ -77,7 +87,7 @@
     first = precondition(resid0)
     resid1 = resid0 - apply_operator(first)
     second = precondition(resid1)
-    top = lax.psum(jnp.sum(resid1 * second, axis=(0, 2)), ("gx", "gy"))
+    top = block_cut(jnp.sum(resid1 * second, axis=(0, 2)))
     curved = apply_operator(second)
     bottom = lax.psum(jnp.sum(second * curved, axis=(0, 2)), ("gx", "gy"))
     step_len = top / bottom

time: 211 us -> 252 us (1.19)
  blocking collectives: 115 us -> 156 us
  waiting for transfers between devices: 16.9 us -> 13.1 us
    psum x1 -> x3, blocking collectives: 45.2 us -> 86.3 us  [the longest x1 47.5 us: per_device(): bottom = lax.psum(jnp.sum(second * curved, axis=(0, 2)), ('gx', 'gy'))]
    ppermute x10, waiting for transfers between devices: 16.8 us -> 13.1 us  [with_halo(): lax.ppermute(lax.slice_in_dim(block, 0, width, axis=dim), axis, backward)]
  transfers between devices with their start and end apart: 20 -> 20, of which waited for: 5 -> 4; matrix products, arithmetic and copies ran while one was open for 1% -> 0% of each run, Pallas kernels for 0% -> 0%
where the time goes in v1:
time: 252 us; the launch traced here: 251 us
  blocking collectives  156 us (62%)
  starting transfers between devices  56.1 us (22%)
  matrix products  15.6 us (6%)
  waiting for transfers between devices  13.1 us (5%)
  local copies, waits for them, and re-layouts  5.08 us (2%)
  other arithmetic  4.35 us (2%)
    all_gather x2, blocking collectives, precondition(): lax.all_gather(primal, ('gx', 'gy'), axis=0, tiled=True)  69.4 us
    psum x1, blocking collectives, per_device(): bottom = lax.psum(jnp.sum(second * curved, axis=(0, 2)), ('gx', 'gy'))  47.5 us
    psum x2, blocking collectives, switch_face_over_axis(): point = jax.lax.psum(point, idx)  38.8 us
    ppermute x10, starting transfers between devices, with_halo(): lax.ppermute(lax.slice_in_dim(block, block.shape[dim] - width, None, axis...  31.7 us
    ppermute x10, starting transfers between devices, with_halo(): lax.ppermute(lax.slice_in_dim(block, 0, width, axis=dim), axis, backward)  24.4 us
    ppermute x10, waiting for transfers between devices, with_halo(): lax.ppermute(lax.slice_in_dim(block, 0, width, axis=dim), axis, backward)  13.1 us
    dot_general x6, matrix products, face_mul(): jnp.einsum('fry,fyx->frx', vectors, matrices, preferred_element_type=jnp....  9.99 us
  transfers between devices with their start and end apart: 20, of which 4 were waited for; matrix products, arithmetic and copies ran while one was open for 0% of the time, Pallas kernels for 0%

profile of v1, /device:TPU:10, one launch (start us, length us, event | category | flops | bytes accessed | tf_op | source)
XLA Modules:
  0.0 250.8 jit_solution(2361604040220817002)
XLA Ops:
  0.0 1.3 slice_bitcast_fusion.3
  1.3 3.4 %collective-permute-start = (bf16[1,192,384]{2,1,0:T(8,128)(2,1)S(1)}, bf16[1,192,384]{2,1,0:T(8,128)(2,1)S(1)}, u32[]{:S(2)}, u32[]{:S(2)}) collective-permute-start(bf16[1,192,384]{2,1,0:T(8,128)(2,1)S(1)} %get-tuple-element.21), channel_id=1, source_target_pairs={{0,2},{2,4},{4,6},{6,8},{8,10},{10,12},{12,14},{14,16},{16,18},{18... | collective-permute-start | bytes 442376 | tf_op jit(solution)/shard_map/ppermute | solution.py:22
  4.7 2.4 collective-permute-start.1
  8.5 3.0 %collective-permute-start.2 = (bf16[1,192,384]{2,1,0:T(8,128)(2,1)S(1)}, bf16[1,192,384]{2,1,0:T(8,128)(2,1)S(1)}, u32[]{:S(2)}, u32[]{:S(2)}) collective-permute-start(bf16[1,192,384]{2,1,0:T(8,128)(2,1)S(1)} %get-tuple-element.24), channel_id=1, source_target_pairs={{0,1},{2,3},{4,5},{6,7},{8,9},{10,11},{12,13},{14,15},{16,17},{18,... | collective-permute-start | bytes 442376 | tf_op jit(solution)/shard_map/ppermute | solution.py:22
  14.0 34.1 %all-gather = bf16[32,4,192]{2,1,0:T(4,128)(2,1)} all-gather(bf16[1,4,192]{2,1,0:T(4,128)(2,1)S(1)} %fusion.25), channel_id=1, replica_groups=mesh['gx'=16,'gy'=2] {'gx','gy'}, dimensions={0}, use_global_device_ids=true | all-gather | bytes 50688 | tf_op jit(solution)/shard_map/all_gather | solution.py:76
  48.0 1.5 reshape.37
  49.6 1.6 fusion.14
  51.2 1.8 convolution_bitcast_fusion.1
  53.0 2.9 %convolution_convert_fusion.4 = bf16[4,192,384]{2,1,0:T(8,128)(2,1)S(1)} fusion(f32[4,192,384]{2,1,0:T(8,128)} %convolution_bitcast_fusion.1, f32[4,192,384]{2,1,0:T(8,128)} %fusion.14, bf16[1,1,4,384,384]{4,3,2,1,0:T(8,128)(2,1)S(1)} %copy-done.1, bf16[1,1,4,384,384]{4,3,2,1,0:T(8,128)(2,1)S(1)} %copy-done, f32[4]{0:T(128)} %multiply_bitcast_fusion), kind=kOutput, calls=%fused_computation.14 | convolution fusion | flops 454754304 | bytes 5308432 | tf_op jit(solution)/shard_map/fry,fyx->frx/dot_general | solution.py:31
  56.0 3.5 %collective-permute-start.4 = (bf16[1,192,384]{2,1,0:T(8,128)(2,1)S(1)}, bf16[1,192,384]{2,1,0:T(8,128)(2,1)S(1)}, u32[]{:S(2)}, u32[]{:S(2)}) collective-permute-start(bf16[1,192,384]{2,1,0:T(8,128)(2,1)S(1)} %get-tuple-element.17), channel_id=1, source_target_pairs={{0,2},{2,4},{4,6},{6,8},{8,10},{10,12},{12,14},{14,16},{16,18},{18... | collective-permute-start | bytes 442376 | tf_op jit(solution)/shard_map/ppermute | solution.py:22
  60.9 3.0 %collective-permute-start.6 = (bf16[1,192,384]{2,1,0:T(8,128)(2,1)S(1)}, bf16[1,192,384]{2,1,0:T(8,128)(2,1)S(1)}, u32[]{:S(2)}, u32[]{:S(2)}) collective-permute-start(bf16[1,192,384]{2,1,0:T(8,128)(2,1)S(1)} %get-tuple-element.19), channel_id=1, source_target_pairs={{0,1},{2,3},{4,5},{6,7},{8,9},{10,11},{12,13},{14,15},{16,17},{18,... | collective-permute-start | bytes 442376 | tf_op jit(solution)/shard_map/ppermute | solution.py:22
  63.9 4.6 %collective-permute-start.5 = (bf16[1,192,384]{2,1,0:T(8,128)(2,1)S(1)}, bf16[1,192,384]{2,1,0:T(8,128)(2,1)S(1)}, u32[]{:S(2)}, u32[]{:S(2)}) collective-permute-start(bf16[1,192,384]{2,1,0:T(8,128)(2,1)S(1)} %get-tuple-element.20), channel_id=1, source_target_pairs={{2,0},{4,2},{6,4},{8,6},{10,8},{12,10},{14,12},{16,14},{18,16},{20... | collective-permute-start | bytes 442376 | tf_op jit(solution)/shard_map/ppermute | solution.py:25
  68.6 3.3 %collective-permute-done.5 = bf16[1,192,384]{2,1,0:T(8,128)(2,1)S(1)} collective-permute-done((bf16[1,192,384]{2,1,0:T(8,128)(2,1)S(1)}, bf16[1,192,384]{2,1,0:T(8,128)(2,1)S(1)}, u32[]{:S(2)}, u32[]{:S(2)}) %collective-permute-start.5) | collective-permute-done | bytes 147488 | tf_op jit(solution)/shard_map/ppermute | solution.py:25
  72.6 3.5 %collective-permute-start.8 = (bf16[1,192,384]{2,1,0:T(8,128)(2,1)S(1)}, bf16[1,192,384]{2,1,0:T(8,128)(2,1)S(1)}, u32[]{:S(2)}, u32[]{:S(2)}) collective-permute-start(bf16[1,192,384]{2,1,0:T(8,128)(2,1)S(1)} %get-tuple-element.13), channel_id=1, source_target_pairs={{0,2},{2,4},{4,6},{6,8},{8,10},{10,12},{12,14},{14,16},{16,18},{18... | collective-permute-start | bytes 442376 | tf_op jit(solution)/shard_map/ppermute | solution.py:22
  77.4 3.0 %collective-permute-start.10 = (bf16[1,192,384]{2,1,0:T(8,128)(2,1)S(1)}, bf16[1,192,384]{2,1,0:T(8,128)(2,1)S(1)}, u32[]{:S(2)}, u32[]{:S(2)}) collective-permute-start(bf16[1,192,384]{2,1,0:T(8,128)(2,1)S(1)} %get-tuple-element.15), channel_id=1, source_target_pairs={{0,1},{2,3},{4,5},{6,7},{8,9},{10,11},{12,13},{14,15},{16,17},{18,... | collective-permute-start | bytes 442376 | tf_op jit(solution)/shard_map/ppermute | solution.py:22
  80.4 3.6 %collective-permute-start.9 = (bf16[1,192,384]{2,1,0:T(8,128)(2,1)S(1)}, bf16[1,192,384]{2,1,0:T(8,128)(2,1)S(1)}, u32[]{:S(2)}, u32[]{:S(2)}) collective-permute-start(bf16[1,192,384]{2,1,0:T(8,128)(2,1)S(1)} %get-tuple-element.16), channel_id=1, source_target_pairs={{2,0},{4,2},{6,4},{8,6},{10,8},{12,10},{14,12},{16,14},{18,16},{20... | collective-permute-start | bytes 442376 | tf_op jit(solution)/shard_map/ppermute | solution.py:25
  84.1 5.0 %collective-permute-done.9 = bf16[1,192,384]{2,1,0:T(8,128)(2,1)S(1)} collective-permute-done((bf16[1,192,384]{2,1,0:T(8,128)(2,1)S(1)}, bf16[1,192,384]{2,1,0:T(8,128)(2,1)S(1)}, u32[]{:S(2)}, u32[]{:S(2)}) %collective-permute-start.9) | collective-permute-done | bytes 147488 | tf_op jit(solution)/shard_map/ppermute | solution.py:25
  90.2 1.6 fusion.10
  91.7 35.3 %all-gather.1 = bf16[32,4,192]{2,1,0:T(4,128)(2,1)S(1)} all-gather(bf16[1,4,192]{2,1,0:T(4,128)(2,1)S(1)} %fusion.24), channel_id=1, replica_groups=mesh['gx'=16,'gy'=2] {'gx','gy'}, dimensions={0}, use_global_device_ids=true | all-gather | bytes 50688 | tf_op jit(solution)/shard_map/all_gather | solution.py:76
  127.3 1.8 convolution_bitcast_fusion
  129.1 2.9 %convolution_convert_fusion.1 = bf16[4,192,384]{2,1,0:T(8,128)(2,1)S(1)} fusion(f32[4,192,384]{2,1,0:T(8,128)} %convolution_bitcast_fusion, f32[4,192,384]{2,1,0:T(8,128)} %fusion.10, bf16[1,1,4,384,384]{4,3,2,1,0:T(8,128)(2,1)S(1)} %copy-done.1, bf16[1,1,4,384,384]{4,3,2,1,0:T(8,128)(2,1)S(1)} %copy-done, f32[4]{0:T(128)} %multiply_bitcast_fusion), kind=kOutput, calls=%fused_computation.11 | convolution fusion | flops 454754304 | bytes 5308432 | tf_op jit(solution)/shard_map/fry,fyx->frx/dot_general | solution.py:31
  132.0 2.1 collective-permute-start.12
  135.4 3.0 %collective-permute-start.14 = (bf16[1,192,384]{2,1,0:T(8,128)(2,1)S(1)}, bf16[1,192,384]{2,1,0:T(8,128)(2,1)S(1)}, u32[]{:S(2)}, u32[]{:S(2)}) collective-permute-start(bf16[1,192,384]{2,1,0:T(8,128)(2,1)S(1)} %get-tuple-element.11), channel_id=1, source_target_pairs={{0,1},{2,3},{4,5},{6,7},{8,9},{10,11},{12,13},{14,15},{16,17},{18,... | collective-permute-start | bytes 442376 | tf_op jit(solution)/shard_map/ppermute | solution.py:22
  138.4 3.9 %collective-permute-start.13 = (bf16[1,192,384]{2,1,0:T(8,128)(2,1)S(1)}, bf16[1,192,384]{2,1,0:T(8,128)(2,1)S(1)}, u32[]{:S(2)}, u32[]{:S(2)}) collective-permute-start(bf16[1,192,384]{2,1,0:T(8,128)(2,1)S(1)} %get-tuple-element.12), channel_id=1, source_target_pairs={{2,0},{4,2},{6,4},{8,6},{10,8},{12,10},{14,12},{16,14},{18,16},{20... | collective-permute-start | bytes 442376 | tf_op jit(solution)/shard_map/ppermute | solution.py:25
  142.4 3.9 %collective-permute-done.13 = bf16[1,192,384]{2,1,0:T(8,128)(2,1)S(1)} collective-permute-done((bf16[1,192,384]{2,1,0:T(8,128)(2,1)S(1)}, bf16[1,192,384]{2,1,0:T(8,128)(2,1)S(1)}, u32[]{:S(2)}, u32[]{:S(2)}) %collective-permute-start.13) | collective-permute-done | bytes 147488 | tf_op jit(solution)/shard_map/ppermute | solution.py:25
  148.7 2.7 %collective-permute-start.16 = (bf16[1,192,384]{2,1,0:T(8,128)(2,1)}, bf16[1,192,384]{2,1,0:T(8,128)(2,1)}, u32[]{:S(2)}, u32[]{:S(2)}) collective-permute-start(bf16[1,192,384]{2,1,0:T(8,128)(2,1)} %get-tuple-element.5), channel_id=1, source_target_pairs={{0,2},{2,4},{4,6},{6,8},{8,10},{10,12},{12,14},{14,16},{16,18},{18... | collective-permute-start | bytes 442376 | tf_op jit(solution)/shard_map/ppermute | solution.py:22
  152.7 4.3 %collective-permute-start.18 = (bf16[1,192,384]{2,1,0:T(8,128)(2,1)}, bf16[1,192,384]{2,1,0:T(8,128)(2,1)}, u32[]{:S(2)}, u32[]{:S(2)}) collective-permute-start(bf16[1,192,384]{2,1,0:T(8,128)(2,1)} %get-tuple-element.7), channel_id=1, source_target_pairs={{0,1},{2,3},{4,5},{6,7},{8,9},{10,11},{12,13},{14,15},{16,17},{18,... | collective-permute-start | bytes 442376 | tf_op jit(solution)/shard_map/ppermute | solution.py:22
  157.0 3.3 %collective-permute-start.17 = (bf16[1,192,384]{2,1,0:T(8,128)(2,1)}, bf16[1,192,384]{2,1,0:T(8,128)(2,1)}, u32[]{:S(2)}, u32[]{:S(2)}) collective-permute-start(bf16[1,192,384]{2,1,0:T(8,128)(2,1)} %get-tuple-element.8), channel_id=1, source_target_pairs={{2,0},{4,2},{6,4},{8,6},{10,8},{12,10},{14,12},{16,14},{18,16},{20... | collective-permute-start | bytes 442376 | tf_op jit(solution)/shard_map/ppermute | solution.py:25
  161.1 2.5 psum.21
  163.6 36.3 %psum.22 = f32[192]{0:T(256)S(1)} all-reduce(f32[192]{0:T(256)S(1)} %psum.21), channel_id=1, replica_groups=mesh['gx'=16,'gy'=2] {'gx'}, use_global_device_ids=true, to_apply=%region_2.0 | all-reduce | flops 192 | bytes 1536 | tf_op jit(solution)/shard_map/psum | solution.py:10
  200.0 2.0 multiply_reduce_fusion
  202.0 47.5 %psum.23 = f32[192]{0:T(256)S(1)} all-reduce(f32[192]{0:T(256)S(1)} %multiply_reduce_fusion), channel_id=1, replica_groups=mesh['gx'=16,'gy'=2] {'gx','gy'}, use_global_device_ids=true, to_apply=%region_4.0 | all-reduce | flops 192 | bytes 1536 | tf_op jit(solution)/shard_map/psum | solution.py:92
  (138 shorter events, 15.0 us)
Async XLA Ops:
  1.3 10.8 %collective-permute-start = (bf16[1,192,384]{2,1,0:T(8,128)(2,1)S(1)}, bf16[1,192,384]{2,1,0:T(8,128)(2,1)S(1)}, u32[]{:S(2)}, u32[]{:S(2)}) collective-permute-start(bf16[1,192,384]{2,1,0:T(8,128)(2,1)S(1)} %get-tuple-element.21), channel_id=1, source_target_pairs={{0,2},{2,4},{4,6},{6,8},{8,10},{10,12},{12,14},{14,16},{16,18},{18... | collective-permute-start | bytes 442376 | tf_op jit(solution)/shard_map/ppermute | solution.py:22
  4.7 8.2 %collective-permute-start.1 = (bf16[1,192,384]{2,1,0:T(8,128)(2,1)S(1)}, bf16[1,192,384]{2,1,0:T(8,128)(2,1)S(1)}, u32[]{:S(2)}, u32[]{:S(2)}) collective-permute-start(bf16[1,192,384]{2,1,0:T(8,128)(2,1)S(1)} %get-tuple-element.22), channel_id=1, source_target_pairs={{2,0},{4,2},{6,4},{8,6},{10,8},{12,10},{14,12},{16,14},{18,16},{20... | collective-permute-start | bytes 442376 | tf_op jit(solution)/shard_map/ppermute | solution.py:25
  7.2 5.7 %collective-permute-start.3 = (bf16[1,192,384]{2,1,0:T(8,128)(2,1)S(1)}, bf16[1,192,384]{2,1,0:T(8,128)(2,1)S(1)}, u32[]{:S(2)}, u32[]{:S(2)}) collective-permute-start(bf16[1,192,384]{2,1,0:T(8,128)(2,1)S(1)} %get-tuple-element.23), channel_id=1, source_target_pairs={{1,0},{3,2},{5,4},{7,6},{9,8},{11,10},{13,12},{15,14},{17,16},{19,... | collective-permute-start | bytes 442376 | tf_op jit(solution)/shard_map/ppermute | solution.py:25
  8.5 4.5 %collective-permute-start.2 = (bf16[1,192,384]{2,1,0:T(8,128)(2,1)S(1)}, bf16[1,192,384]{2,1,0:T(8,128)(2,1)S(1)}, u32[]{:S(2)}, u32[]{:S(2)}) collective-permute-start(bf16[1,192,384]{2,1,0:T(8,128)(2,1)S(1)} %get-tuple-element.24), channel_id=1, source_target_pairs={{0,1},{2,3},{4,5},{6,7},{8,9},{10,11},{12,13},{14,15},{16,17},{18,... | collective-permute-start | bytes 442376 | tf_op jit(solution)/shard_map/ppermute | solution.py:22
  13.0 36.6 %copy-start.1 = (bf16[1,1,4,384,384]{4,3,2,1,0:T(8,128)(2,1)S(1)}, bf16[1,1,4,384,384]{4,3,2,1,0:T(8,128)(2,1)}, u32[]{:S(2)}) copy-start(bf16[1,1,4,384,384]{4,3,2,1,0:T(8,128)(2,1)} %param.10) | copy-start | bytes 3538948
  56.0 12.5 %collective-permute-start.4 = (bf16[1,192,384]{2,1,0:T(8,128)(2,1)S(1)}, bf16[1,192,384]{2,1,0:T(8,128)(2,1)S(1)}, u32[]{:S(2)}, u32[]{:S(2)}) collective-permute-start(bf16[1,192,384]{2,1,0:T(8,128)(2,1)S(1)} %get-tuple-element.17), channel_id=1, source_target_pairs={{0,2},{2,4},{4,6},{6,8},{8,10},{10,12},{12,14},{14,16},{16,18},{18... | collective-permute-start | bytes 442376 | tf_op jit(solution)/shard_map/ppermute | solution.py:22
  59.6 9.0 %collective-permute-start.7 = (bf16[1,192,384]{2,1,0:T(8,128)(2,1)S(1)}, bf16[1,192,384]{2,1,0:T(8,128)(2,1)S(1)}, u32[]{:S(2)}, u32[]{:S(2)}) collective-permute-start(bf16[1,192,384]{2,1,0:T(8,128)(2,1)S(1)} %get-tuple-element.18), channel_id=1, source_target_pairs={{1,0},{3,2},{5,4},{7,6},{9,8},{11,10},{13,12},{15,14},{17,16},{19,... | collective-permute-start | bytes 442376 | tf_op jit(solution)/shard_map/ppermute | solution.py:25
  60.9 7.7 %collective-permute-start.6 = (bf16[1,192,384]{2,1,0:T(8,128)(2,1)S(1)}, bf16[1,192,384]{2,1,0:T(8,128)(2,1)S(1)}, u32[]{:S(2)}, u32[]{:S(2)}) collective-permute-start(bf16[1,192,384]{2,1,0:T(8,128)(2,1)S(1)} %get-tuple-element.19), channel_id=1, source_target_pairs={{0,1},{2,3},{4,5},{6,7},{8,9},{10,11},{12,13},{14,15},{16,17},{18,... | collective-permute-start | bytes 442376 | tf_op jit(solution)/shard_map/ppermute | solution.py:22
  63.9 7.9 %collective-permute-start.5 = (bf16[1,192,384]{2,1,0:T(8,128)(2,1)S(1)}, bf16[1,192,384]{2,1,0:T(8,128)(2,1)S(1)}, u32[]{:S(2)}, u32[]{:S(2)}) collective-permute-start(bf16[1,192,384]{2,1,0:T(8,128)(2,1)S(1)} %get-tuple-element.20), channel_id=1, source_target_pairs={{2,0},{4,2},{6,4},{8,6},{10,8},{12,10},{14,12},{16,14},{18,16},{20... | collective-permute-start | bytes 442376 | tf_op jit(solution)/shard_map/ppermute | solution.py:25
  72.6 11.5 %collective-permute-start.8 = (bf16[1,192,384]{2,1,0:T(8,128)(2,1)S(1)}, bf16[1,192,384]{2,1,0:T(8,128)(2,1)S(1)}, u32[]{:S(2)}, u32[]{:S(2)}) collective-permute-start(bf16[1,192,384]{2,1,0:T(8,128)(2,1)S(1)} %get-tuple-element.13), channel_id=1, source_target_pairs={{0,2},{2,4},{4,6},{6,8},{8,10},{10,12},{12,14},{14,16},{16,18},{18... | collective-permute-start | bytes 442376 | tf_op jit(solution)/shard_map/ppermute | solution.py:22
  76.1 8.0 %collective-permute-start.11 = (bf16[1,192,384]{2,1,0:T(8,128)(2,1)S(1)}, bf16[1,192,384]{2,1,0:T(8,128)(2,1)S(1)}, u32[]{:S(2)}, u32[]{:S(2)}) collective-permute-start(bf16[1,192,384]{2,1,0:T(8,128)(2,1)S(1)} %get-tuple-element.14), channel_id=1, source_target_pairs={{1,0},{3,2},{5,4},{7,6},{9,8},{11,10},{13,12},{15,14},{17,16},{19,... | collective-permute-start | bytes 442376 | tf_op jit(solution)/shard_map/ppermute | solution.py:25
  77.4 6.7 %collective-permute-start.10 = (bf16[1,192,384]{2,1,0:T(8,128)(2,1)S(1)}, bf16[1,192,384]{2,1,0:T(8,128)(2,1)S(1)}, u32[]{:S(2)}, u32[]{:S(2)}) collective-permute-start(bf16[1,192,384]{2,1,0:T(8,128)(2,1)S(1)} %get-tuple-element.15), channel_id=1, source_target_pairs={{0,1},{2,3},{4,5},{6,7},{8,9},{10,11},{12,13},{14,15},{16,17},{18,... | collective-permute-start | bytes 442376 | tf_op jit(solution)/shard_map/ppermute | solution.py:22
  80.4 8.7 %collective-permute-start.9 = (bf16[1,192,384]{2,1,0:T(8,128)(2,1)S(1)}, bf16[1,192,384]{2,1,0:T(8,128)(2,1)S(1)}, u32[]{:S(2)}, u32[]{:S(2)}) collective-permute-start(bf16[1,192,384]{2,1,0:T(8,128)(2,1)S(1)} %get-tuple-element.16), channel_id=1, source_target_pairs={{2,0},{4,2},{6,4},{8,6},{10,8},{12,10},{14,12},{16,14},{18,16},{20... | collective-permute-start | bytes 442376 | tf_op jit(solution)/shard_map/ppermute | solution.py:25
  132.0 10.3 %collective-permute-start.12 = (bf16[1,192,384]{2,1,0:T(8,128)(2,1)S(1)}, bf16[1,192,384]{2,1,0:T(8,128)(2,1)S(1)}, u32[]{:S(2)}, u32[]{:S(2)}) collective-permute-start(bf16[1,192,384]{2,1,0:T(8,128)(2,1)S(1)} %get-tuple-element.9), channel_id=1, source_target_pairs={{0,2},{2,4},{4,6},{6,8},{8,10},{10,12},{12,14},{14,16},{16,18},{18... | collective-permute-start | bytes 442376 | tf_op jit(solution)/shard_map/ppermute | solution.py:22
  134.1 8.3 %collective-permute-start.15 = (bf16[1,192,384]{2,1,0:T(8,128)(2,1)S(1)}, bf16[1,192,384]{2,1,0:T(8,128)(2,1)S(1)}, u32[]{:S(2)}, u32[]{:S(2)}) collective-permute-start(bf16[1,192,384]{2,1,0:T(8,128)(2,1)S(1)} %get-tuple-element.10), channel_id=1, source_target_pairs={{1,0},{3,2},{5,4},{7,6},{9,8},{11,10},{13,12},{15,14},{17,16},{19,... | collective-permute-start | bytes 442376 | tf_op jit(solution)/shard_map/ppermute | solution.py:25
  135.4 7.0 %collective-permute-start.14 = (bf16[1,192,384]{2,1,0:T(8,128)(2,1)S(1)}, bf16[1,192,384]{2,1,0:T(8,128)(2,1)S(1)}, u32[]{:S(2)}, u32[]{:S(2)}) collective-permute-start(bf16[1,192,384]{2,1,0:T(8,128)(2,1)S(1)} %get-tuple-element.11), channel_id=1, source_target_pairs={{0,1},{2,3},{4,5},{6,7},{8,9},{10,11},{12,13},{14,15},{16,17},{18,... | collective-permute-start | bytes 442376 | tf_op jit(solution)/shard_map/ppermute | solution.py:22
  138.4 7.9 %collective-permute-start.13 = (bf16[1,192,384]{2,1,0:T(8,128)(2,1)S(1)}, bf16[1,192,384]{2,1,0:T(8,128)(2,1)S(1)}, u32[]{:S(2)}, u32[]{:S(2)}) collective-permute-start(bf16[1,192,384]{2,1,0:T(8,128)(2,1)S(1)} %get-tuple-element.12), channel_id=1, source_target_pairs={{2,0},{4,2},{6,4},{8,6},{10,8},{12,10},{14,12},{16,14},{18,16},{20... | collective-permute-start | bytes 442376 | tf_op jit(solution)/shard_map/ppermute | solution.py:25
  142.4 18.0 %copy-start.7 = (bf16[1,192,384]{2,1,0:T(8,128)(2,1)}, bf16[1,192,384]{2,1,0:T(8,128)(2,1)S(1)}, u32[]{:S(2)}) copy-start(bf16[1,192,384]{2,1,0:T(8,128)(2,1)S(1)} %collective-permute-done.12) | copy-start | bytes 442372
  142.4 18.0 %copy-start.9 = (bf16[1,192,384]{2,1,0:T(8,128)(2,1)}, bf16[1,192,384]{2,1,0:T(8,128)(2,1)S(1)}, u32[]{:S(2)}) copy-start(bf16[1,192,384]{2,1,0:T(8,128)(2,1)S(1)} %collective-permute-done.15) | copy-start | bytes 442372
  142.4 18.0 %copy-start.11 = (bf16[1,192,384]{2,1,0:T(8,128)(2,1)}, bf16[1,192,384]{2,1,0:T(8,128)(2,1)S(1)}, u32[]{:S(2)}) copy-start(bf16[1,192,384]{2,1,0:T(8,128)(2,1)S(1)} %collective-permute-done.14) | copy-start | bytes 442372
  148.7 51.2 %collective-permute-start.16 = (bf16[1,192,384]{2,1,0:T(8,128)(2,1)}, bf16[1,192,384]{2,1,0:T(8,128)(2,1)}, u32[]{:S(2)}, u32[]{:S(2)}) collective-permute-start(bf16[1,192,384]{2,1,0:T(8,128)(2,1)} %get-tuple-element.5), channel_id=1, source_target_pairs={{0,2},{2,4},{4,6},{6,8},{8,10},{10,12},{12,14},{14,16},{16,18},{18... | collective-permute-start | bytes 442376 | tf_op jit(solution)/shard_map/ppermute | solution.py:22
  151.4 48.5 %collective-permute-start.19 = (bf16[1,192,384]{2,1,0:T(8,128)(2,1)}, bf16[1,192,384]{2,1,0:T(8,128)(2,1)}, u32[]{:S(2)}, u32[]{:S(2)}) collective-permute-start(bf16[1,192,384]{2,1,0:T(8,128)(2,1)} %get-tuple-element.6), channel_id=1, source_target_pairs={{1,0},{3,2},{5,4},{7,6},{9,8},{11,10},{13,12},{15,14},{17,16},{19,... | collective-permute-start | bytes 442376 | tf_op jit(solution)/shard_map/ppermute | solution.py:25
  152.7 47.2 %collective-permute-start.18 = (bf16[1,192,384]{2,1,0:T(8,128)(2,1)}, bf16[1,192,384]{2,1,0:T(8,128)(2,1)}, u32[]{:S(2)}, u32[]{:S(2)}) collective-permute-start(bf16[1,192,384]{2,1,0:T(8,128)(2,1)} %get-tuple-element.7), channel_id=1, source_target_pairs={{0,1},{2,3},{4,5},{6,7},{8,9},{10,11},{12,13},{14,15},{16,17},{18,... | collective-permute-start | bytes 442376 | tf_op jit(solution)/shard_map/ppermute | solution.py:22
  157.0 42.9 %collective-permute-start.17 = (bf16[1,192,384]{2,1,0:T(8,128)(2,1)}, bf16[1,192,384]{2,1,0:T(8,128)(2,1)}, u32[]{:S(2)}, u32[]{:S(2)}) collective-permute-start(bf16[1,192,384]{2,1,0:T(8,128)(2,1)} %get-tuple-element.8), channel_id=1, source_target_pairs={{2,0},{4,2},{6,4},{8,6},{10,8},{12,10},{14,12},{16,14},{18,16},{20... | collective-permute-start | bytes 442376 | tf_op jit(solution)/shard_map/ppermute | solution.py:25
  199.9 49.6 %copy-start.8 = (bf16[1,192,384]{2,1,0:T(8,128)(2,1)S(1)}, bf16[1,192,384]{2,1,0:T(8,128)(2,1)}, u32[]{:S(2)}) copy-start(bf16[1,192,384]{2,1,0:T(8,128)(2,1)} %copy-done.7) | copy-start | bytes 442372
  199.9 49.6 %copy-start.10 = (bf16[1,192,384]{2,1,0:T(8,128)(2,1)S(1)}, bf16[1,192,384]{2,1,0:T(8,128)(2,1)}, u32[]{:S(2)}) copy-start(bf16[1,192,384]{2,1,0:T(8,128)(2,1)} %copy-done.9) | copy-start | bytes 442372
  199.9 49.7 %copy-start.12 = (bf16[1,192,384]{2,1,0:T(8,128)(2,1)S(1)}, bf16[1,192,384]{2,1,0:T(8,128)(2,1)}, u32[]{:S(2)}) copy-start(bf16[1,192,384]{2,1,0:T(8,128)(2,1)} %copy-done.11) | copy-start | bytes 442372
  199.9 49.7 %copy-start.14 = (bf16[1,192,384]{2,1,0:T(8,128)(2,1)S(1)}, bf16[1,192,384]{2,1,0:T(8,128)(2,1)}, u32[]{:S(2)}) copy-start(bf16[1,192,384]{2,1,0:T(8,128)(2,1)} %copy-done.13) | copy-start | bytes 442372
  199.9 49.7 %copy-start.29 = (bf16[1,192,384]{2,1,0:T(8,128)(2,1)S(1)}, bf16[1,192,384]{2,1,0:T(8,128)(2,1)}, u32[]{:S(2)}) copy-start(bf16[1,192,384]{2,1,0:T(8,128)(2,1)} %copy-done.28) | copy-start | bytes 442372
  199.9 49.7 %copy-start.31 = (bf16[1,192,384]{2,1,0:T(8,128)(2,1)S(1)}, bf16[1,192,384]{2,1,0:T(8,128)(2,1)}, u32[]{:S(2)}) copy-start(bf16[1,192,384]{2,1,0:T(8,128)(2,1)} %copy-done.30) | copy-start | bytes 442372
  199.9 49.7 %copy-start.33 = (bf16[1,192,384]{2,1,0:T(8,128)(2,1)S(1)}, bf16[1,192,384]{2,1,0:T(8,128)(2,1)}, u32[]{:S(2)}) copy-start(bf16[1,192,384]{2,1,0:T(8,128)(2,1)} %copy-done.32) | copy-start | bytes 442372
  199.9 49.7 %copy-start.35 = (bf16[1,192,384]{2,1,0:T(8,128)(2,1)S(1)}, bf16[1,192,384]{2,1,0:T(8,128)(2,1)}, u32[]{:S(2)}) copy-start(bf16[1,192,384]{2,1,0:T(8,128)(2,1)} %copy-done.34) | copy-start | bytes 442372
  (37 other events, 343.2 us)
